TPU v7x, 256 devices: a whole 4x4x8 slice. The times are simulated.
256 devices in a mesh: ctx: 32 (over z, x), tp: 8 (over y, core).
Axes of the slice: x: 4, y: 4, z: 8, core: 2. Of those that a mesh axis runs over, the one named last changes fastest.
Arguments:
- tokens: bfloat16 [16384, 3072], P(('ctx', 'tp')), may hold values from -6 to 6
- w_query: bfloat16 [3072, 4096], P(None, 'tp'), may hold values from -0.109375 to 0.109375
- w_key: bfloat16 [3072, 4096], P(None, 'tp'), may hold values from -0.109375 to 0.109375
- w_value: bfloat16 [3072, 4096], P(None, 'tp'), may hold values from -0.109375 to 0.109375
- norm_gain: float32 [4096], P('tp'), may hold values from 0.1 to 1.9
Outputs:
- attended: bfloat16 [16384, 4096], P('ctx', 'tp')
All inputs are finite; a program needn't handle non-finite values.
Results may differ from a plain program's by a relative error of at most 0.0062.
Values may be sent and summed in bfloat16 or wider, within the bound.
No kernel may reach another device: no remote copies, remote signals or barrier semaphores. Data moves between devices by JAX's collectives and lax.ppermute only.
A program may use at most 64 MiB of HBM per device.

v0:
```python
import jax
import jax.numpy as jnp
from jax import lax
from jax.sharding import PartitionSpec as P

HEAD_DIM = 128
BLOCK = 512
EPSILON = 1e-06


def from_behind(value, axis, by):
    size = lax.axis_size(axis)
    pairs = [(i, i + by) for i in range(size) if 0 <= i + by < size]
    return lax.ppermute(value, axis, pairs)


def exclusive_scan(value, axis):
    size = lax.axis_size(axis)
    covered = value
    before = None
    by = 1
    while by < size:
        piece = from_behind(covered, axis, by)
        before = piece if before is None else before + piece
        by *= 2
        if by < size:
            covered = covered + piece
    return before


def body(tokens, w_query, w_key, w_value, norm_gain):
    local_width = w_query.shape[1]
    head_count = local_width // HEAD_DIM
    piece_rows = lax.all_gather(tokens, "tp", axis=0, tiled=True)
    query_part = jnp.dot(piece_rows, w_query, preferred_element_type=jnp.float32).astype(
        jnp.bfloat16
    )
    key_part = jnp.dot(piece_rows, w_key, preferred_element_type=jnp.float32).astype(jnp.bfloat16)
    value_part = jnp.dot(piece_rows, w_value, preferred_element_type=jnp.float32).astype(
        jnp.bfloat16
    )
    projected = jnp.concatenate([query_part, key_part, value_part], axis=1)
    group_len = projected.shape[0]
    block_count = group_len // BLOCK
    shaped = projected.reshape(block_count, BLOCK, 3, head_count, HEAD_DIM)
    query_rows = shaped[:, :, 0]
    key_rows = shaped[:, :, 1]
    value_rows = shaped[:, :, 2]
    block_states = jnp.einsum(
        "bshd,bshe->bhde", key_rows, value_rows, preferred_element_type=jnp.float32
    )
    local_state = jnp.sum(block_states, axis=0)
    prefix_state = exclusive_scan(local_state, "ctx")
    running = jnp.cumsum(block_states, axis=0)
    earlier = jnp.concatenate([jnp.zeros_like(block_states), running[:-1]], axis=0)
    block_start = prefix_state[None] + earlier
    scores = jnp.einsum("bqhd,bkhd->bhqk", query_rows, key_rows, preferred_element_type=jnp.float32)
    causal = jnp.arange(BLOCK)[:, None] >= jnp.arange(BLOCK)[None, :]
    scores = jnp.where(causal[None, None], scores, jnp.float32(0.0)).astype(jnp.bfloat16)
    inner = jnp.einsum("bhqk,bkhe->bqhe", scores, value_rows, preferred_element_type=jnp.float32)
    carried_part = jnp.einsum(
        "bqhd,bhde->bqhe",
        query_rows.astype(jnp.float32),
        block_start,
        precision=lax.Precision.HIGHEST,
    )
    mixed = inner + carried_part
    mean_square = jnp.mean(mixed * mixed, axis=-1, keepdims=True)
    normed = mixed * lax.rsqrt(mean_square + EPSILON) * norm_gain.reshape(head_count, HEAD_DIM)
    return normed.reshape(group_len, local_width).astype(jnp.bfloat16)


def solution(mesh):
    placed = (P(("ctx", "tp"), None), P(None, "tp"), P(None, "tp"), P(None, "tp"), P("tp"))
    return jax.shard_map(
        body, mesh=mesh, in_specs=placed, out_specs=P("ctx", "tp"), check_vma=False
    )
```

profile of v0, /device:TPU:192, one launch (start us, length us, event | category | flops | bytes accessed | tf_op | source)
XLA Modules:
  0.0 132.0 jit_solution(15375087548146200491)
XLA Ops:
  6.5 0.0 copy-start
  6.5 0.0 all-gather.2.cloned.1.call-start
  6.5 0.7 all-gather.2.cloned.1.call-update
  7.3 33.0 %all-gather.2.cloned.1.call-done = bf16[512,3072]{1,0:T(8,128)(2,1)} async-done(((bf16[64,3072]{1,0:T(8,128)(2,1)}), bf16[512,3072]{1,0:T(8,128)(2,1)}) %all-gather.2.cloned.1.call-update) | async-done | bytes 3145744 | tf_op jit(solution)/shard_map/all_gather | solution.py:34
  40.3 0.0 copy-done
  40.3 0.0 copy-start.6
  40.3 0.0 copy-start.8
  40.3 3.9 %convolution_convert_fusion = bf16[512,512]{0,1:T(8,128)(2,1)S(1)} fusion(bf16[512,3072]{1,0:T(8,128)(2,1)} %all-gather.2.cloned.1.call-done, bf16[3072,512]{1,0:T(8,128)(2,1)S(1)} %copy-done), kind=kOutput, calls=%fused_computation.5 | convolution fusion | flops 1610874880 | bytes 6815744 | tf_op jit(solution)/shard_map/dot_general | solution.py:39
  44.1 0.0 copy-done.6
  44.1 0.0 copy-done.8
  44.2 0.0 copy-start.7
  44.2 1.8 %convolution_convert_fusion.1 = bf16[512,512]{0,1:T(8,128)(2,1)S(1)} fusion(bf16[512,3072]{1,0:T(8,128)(2,1)S(1)} %copy-done.8, bf16[3072,512]{1,0:T(8,128)(2,1)S(1)} %copy-done.6), kind=kOutput, calls=%fused_computation.6 | convolution fusion | flops 1610874880 | bytes 6815744 | tf_op jit(solution)/shard_map/dot_general | solution.py:38
  46.0 0.0 copy-done.7
  46.1 1.8 %convolution_convert_fusion.2 = bf16[512,512]{0,1:T(8,128)(2,1)S(1)} fusion(bf16[512,3072]{1,0:T(8,128)(2,1)S(1)} %copy-done.8, bf16[3072,512]{1,0:T(8,128)(2,1)S(1)} %copy-done.7), kind=kOutput, calls=%fused_computation.7 | convolution fusion | flops 1610874880 | bytes 6815744 | tf_op jit(solution)/shard_map/dot_general | solution.py:35
  47.9 0.1 pad_maximum_fusion
  48.0 0.0 copy-start.1
  48.0 1.2 copy-done.1
  49.2 0.3 fusion.2
  49.5 3.4 %collective-permute-start = (f32[4,128,128]{2,1,0:T(8,128)S(1)}, f32[4,128,128]{2,1,0:T(8,128)S(1)}, u32[]{:S(2)}, u32[]{:S(2)}) collective-permute-start(f32[4,128,128]{2,1,0:T(8,128)S(1)} %fusion.2), channel_id=1, source_target_pairs={{0,8},{8,16},{16,24},{24,32},{32,40},{40,48},{48,56},{56,64},{64,7... | collective-permute-start | bytes 786440 | tf_op jit(solution)/shard_map/ppermute | solution.py:14
  52.8 9.1 %collective-permute-done = f32[4,128,128]{2,1,0:T(8,128)S(1)} collective-permute-done((f32[4,128,128]{2,1,0:T(8,128)S(1)}, f32[4,128,128]{2,1,0:T(8,128)S(1)}, u32[]{:S(2)}, u32[]{:S(2)}) %collective-permute-start) | collective-permute-done | bytes 262176 | tf_op jit(solution)/shard_map/ppermute | solution.py:14
  61.9 2.8 %collective-permute-start.1 = (f32[4,128,128]{2,1,0:T(8,128)S(1)}, f32[4,128,128]{2,1,0:T(8,128)S(1)}, u32[]{:S(2)}, u32[]{:S(2)}) collective-permute-start(f32[4,128,128]{2,1,0:T(8,128)S(1)} %add.44), channel_id=1, source_target_pairs={{0,16},{8,24},{16,32},{24,40},{32,48},{40,56},{48,64},{56,72},{64,... | collective-permute-start | bytes 786440 | tf_op jit(solution)/shard_map/ppermute | solution.py:14
  64.7 9.1 %collective-permute-done.1 = f32[4,128,128]{2,1,0:T(8,128)S(1)} collective-permute-done((f32[4,128,128]{2,1,0:T(8,128)S(1)}, f32[4,128,128]{2,1,0:T(8,128)S(1)}, u32[]{:S(2)}, u32[]{:S(2)}) %collective-permute-start.1) | collective-permute-done | bytes 262176 | tf_op jit(solution)/shard_map/ppermute | solution.py:14
  73.8 0.0 copy-start.2
  73.9 2.6 %collective-permute-start.2 = (f32[4,128,128]{2,1,0:T(8,128)S(1)}, f32[4,128,128]{2,1,0:T(8,128)S(1)}, u32[]{:S(2)}, u32[]{:S(2)}) collective-permute-start(f32[4,128,128]{2,1,0:T(8,128)S(1)} %add.46), channel_id=1, source_target_pairs={{0,32},{8,40},{16,48},{24,56},{32,64},{40,72},{48,80},{56,88},{64,... | collective-permute-start | bytes 786440 | tf_op jit(solution)/shard_map/ppermute | solution.py:14
  76.4 6.1 %collective-permute-done.2 = f32[4,128,128]{2,1,0:T(8,128)S(1)} collective-permute-done((f32[4,128,128]{2,1,0:T(8,128)S(1)}, f32[4,128,128]{2,1,0:T(8,128)S(1)}, u32[]{:S(2)}, u32[]{:S(2)}) %collective-permute-start.2) | collective-permute-done | bytes 262176 | tf_op jit(solution)/shard_map/ppermute | solution.py:14
  82.5 0.0 copy-start.3
  82.5 1.3 collective-permute-start.3
  83.8 0.8 iota_compare_fusion
  84.6 15.5 %collective-permute-done.3 = f32[4,128,128]{2,1,0:T(8,128)S(1)} collective-permute-done((f32[4,128,128]{2,1,0:T(8,128)S(1)}, f32[4,128,128]{2,1,0:T(8,128)S(1)}, u32[]{:S(2)}, u32[]{:S(2)}) %collective-permute-start.3) | collective-permute-done | bytes 262176 | tf_op jit(solution)/shard_map/ppermute | solution.py:14
  100.1 0.0 copy-start.4
  100.1 0.8 add.50
  100.9 0.0 copy-done.2
  100.9 0.0 copy-done.3
  100.9 0.0 copy-done.4
  100.9 1.3 collective-permute-start.4
  102.2 3.8 %fusion = f32[4,128,512]{2,1,0:T(8,128)} fusion(pred[512,512]{1,0:T(8,128)(4,1)} %iota_compare_fusion, bf16[1,512,3,4,128]{1,4,3,2,0:T(8,128)(2,1)} %bitcast.30), kind=kOutput, calls=%fused_computation.1 | convolution fusion | flops 538968064 | bytes 2883584 | tf_op jit(solution)/shard_map/bhqk,bkhe->bqhe/dot_general | solution.py:60
  106.0 0.0 copy-start.5
  106.0 13.7 %collective-permute-done.4 = f32[4,128,128]{2,1,0:T(8,128)} collective-permute-done((f32[4,128,128]{2,1,0:T(8,128)}, f32[4,128,128]{2,1,0:T(8,128)}, u32[]{:S(2)}, u32[]{:S(2)}) %collective-permute-start.4) | collective-permute-done | bytes 262176 | tf_op jit(solution)/shard_map/ppermute | solution.py:14
  119.7 2.4 %multiply_reduce_fusion = (f32[512,4]{0,1:T(4,128)S(1)}, f32[1,512,4,128]{1,3,2,0:T(8,128)S(1)}) fusion(f32[4,128,512]{2,1,0:T(8,128)} %fusion, bf16[1,512,3,4,128]{1,4,3,2,0:T(8,128)(2,1)} %bitcast.31, f32[4,128,128]{2,1,0:T(8,128)} %collective-permute-done.4, f32[4,128,128]{2,1,0:T(8,128)} %copy-done.4, f32[4,128,128]{2,1,0:T(8,128)} %copy-done.3, ...), kind=kOutput, calls=%fused_computation.9 | convolution fusion | flops 403699712 | bytes 3940352 | tf_op jit(solution)/shard_map/bqhd,bhde->bqhe/dot_general | solution.py:61
  122.1 0.0 copy-done.5
  122.1 0.9 multiply_convert_fusion
  123.1 2.0 %copy.9 = bf16[512,512]{1,0:T(8,128)(2,1)} copy(bf16[512,512]{0,1:T(8,128)(2,1)} %bitcast.32) | data formatting | bytes 1048576 | tf_op jit(solution)/shard_map/convert_element_type | solution.py:70
  (4 shorter events, 0.1 us)
Async XLA Ops:
  6.5 33.7 %copy-start = (bf16[3072,512]{1,0:T(8,128)(2,1)S(1)}, bf16[3072,512]{1,0:T(8,128)(2,1)}, u32[]{:S(2)}) copy-start(bf16[3072,512]{1,0:T(8,128)(2,1)} %param.8) | copy-start | bytes 9437188
  6.5 33.7 %all-gather.2.cloned.1.call-start = ((), (), s32[]{:S(2)}) async-start(), calls=%async_computation | async-start | bytes 3538944 | tf_op jit(solution)/shard_map/all_gather | solution.py:34
  40.3 3.9 %copy-start.6 = (bf16[3072,512]{1,0:T(8,128)(2,1)S(1)}, bf16[3072,512]{1,0:T(8,128)(2,1)}, u32[]{:S(2)}) copy-start(bf16[3072,512]{1,0:T(8,128)(2,1)} %param.7) | copy-start | bytes 9437188
  40.3 3.9 %copy-start.8 = (bf16[512,3072]{1,0:T(8,128)(2,1)S(1)}, bf16[512,3072]{1,0:T(8,128)(2,1)}, u32[]{:S(2)}) copy-start(bf16[512,3072]{1,0:T(8,128)(2,1)} %all-gather.2.cloned.1.call-done) | copy-start | bytes 9437188
  44.2 1.9 %copy-start.7 = (bf16[3072,512]{1,0:T(8,128)(2,1)S(1)}, bf16[3072,512]{1,0:T(8,128)(2,1)}, u32[]{:S(2)}) copy-start(bf16[3072,512]{1,0:T(8,128)(2,1)} %param.6) | copy-start | bytes 9437188
  48.0 1.2 copy-start.1
  49.5 12.5 %collective-permute-start = (f32[4,128,128]{2,1,0:T(8,128)S(1)}, f32[4,128,128]{2,1,0:T(8,128)S(1)}, u32[]{:S(2)}, u32[]{:S(2)}) collective-permute-start(f32[4,128,128]{2,1,0:T(8,128)S(1)} %fusion.2), channel_id=1, source_target_pairs={{0,8},{8,16},{16,24},{24,32},{32,40},{40,48},{48,56},{56,64},{64,7... | collective-permute-start | bytes 786440 | tf_op jit(solution)/shard_map/ppermute | solution.py:14
  61.9 11.9 %collective-permute-start.1 = (f32[4,128,128]{2,1,0:T(8,128)S(1)}, f32[4,128,128]{2,1,0:T(8,128)S(1)}, u32[]{:S(2)}, u32[]{:S(2)}) collective-permute-start(f32[4,128,128]{2,1,0:T(8,128)S(1)} %add.44), channel_id=1, source_target_pairs={{0,16},{8,24},{16,32},{24,40},{32,48},{40,56},{48,64},{56,72},{64,... | collective-permute-start | bytes 786440 | tf_op jit(solution)/shard_map/ppermute | solution.py:14
  73.8 27.1 %copy-start.2 = (f32[4,128,128]{2,1,0:T(8,128)}, f32[4,128,128]{2,1,0:T(8,128)S(1)}, u32[]{:S(2)}) copy-start(f32[4,128,128]{2,1,0:T(8,128)S(1)} %collective-permute-done.1) | copy-start | bytes 786436
  73.9 8.6 %collective-permute-start.2 = (f32[4,128,128]{2,1,0:T(8,128)S(1)}, f32[4,128,128]{2,1,0:T(8,128)S(1)}, u32[]{:S(2)}, u32[]{:S(2)}) collective-permute-start(f32[4,128,128]{2,1,0:T(8,128)S(1)} %add.46), channel_id=1, source_target_pairs={{0,32},{8,40},{16,48},{24,56},{32,64},{40,72},{48,80},{56,88},{64,... | collective-permute-start | bytes 786440 | tf_op jit(solution)/shard_map/ppermute | solution.py:14
  82.5 18.4 %copy-start.3 = (f32[4,128,128]{2,1,0:T(8,128)}, f32[4,128,128]{2,1,0:T(8,128)S(1)}, u32[]{:S(2)}) copy-start(f32[4,128,128]{2,1,0:T(8,128)S(1)} %collective-permute-done.2) | copy-start | bytes 786436
  82.5 17.6 %collective-permute-start.3 = (f32[4,128,128]{2,1,0:T(8,128)S(1)}, f32[4,128,128]{2,1,0:T(8,128)S(1)}, u32[]{:S(2)}, u32[]{:S(2)}) collective-permute-start(f32[4,128,128]{2,1,0:T(8,128)S(1)} %add.48), channel_id=1, source_target_pairs={{0,64},{8,72},{16,80},{24,88},{32,96},{40,104},{48,112},{56,120},{... | collective-permute-start | bytes 786440 | tf_op jit(solution)/shard_map/ppermute | solution.py:14
  100.1 0.8 copy-start.4
  100.9 18.8 %collective-permute-start.4 = (f32[4,128,128]{2,1,0:T(8,128)}, f32[4,128,128]{2,1,0:T(8,128)}, u32[]{:S(2)}, u32[]{:S(2)}) collective-permute-start(f32[4,128,128]{2,1,0:T(8,128)} %add.50), channel_id=1, source_target_pairs={{0,128},{8,136},{16,144},{24,152},{32,160},{40,168},{48,176},{56,1... | collective-permute-start | bytes 786440 | tf_op jit(solution)/shard_map/ppermute | solution.py:14
  106.0 16.1 %copy-start.5 = (f32[512]{0:T(512)S(1)}, f32[512]{0:T(512)}, u32[]{:S(2)}) copy-start(f32[512]{0:T(512)} %param.9) | copy-start | bytes 6148
Sparse Core Ops, SparseCore 0:
  9.2 31.0 all-gather.1
where the time goes:
time: 132 us
  waiting for transfers between devices  87.1 us (66%)
  matrix products  14 us (11%)
  between operations  13.5 us (10%)
  starting transfers between devices  11.3 us (9%)
  local copies, waits for them, and re-layouts  3.27 us (2%)
  other arithmetic  2.72 us (2%)
    ppermute x5, waiting for transfers between devices, from_behind(): return lax.ppermute(value, axis, pairs)  53.4 us
    all_gather x1, waiting for transfers between devices, body(): piece_rows = lax.all_gather(tokens, 'tp', axis=0, tiled=True)  33 us
    ppermute x5, starting transfers between devices, from_behind(): return lax.ppermute(value, axis, pairs)  11.3 us
    dot_general x1, matrix products, body(): jnp.dot(piece_rows, w_value, preferred_element_type=jnp.float32)  3.87 us
    dot_general x1, matrix products, body(): jnp.einsum('bhqk,bkhe->bqhe', scores, value_rows, preferred_element_type=...  3.8 us
  transfers between devices with their start and end apart: 6, of which 6 were waited for; matrix products, arithmetic and copies ran while one was open for 3% of the time, Pallas kernels for 0%

commit v1 on v0

--- a/solution.py
+++ b/solution.py
@@ -1,3 +1,4 @@
+import functools
 import jax
 import jax.numpy as jnp
 from jax import lax
@@ -6,6 +7,15 @@
 HEAD_DIM = 128
 BLOCK = 512
 EPSILON = 1e-06
+
+
+def _store_stocks(z, mesh_name):
+    right_arr = jnp.stack([z for _ in range(lax.axis_size(mesh_name))], axis=0)
+    z1 = lax.all_to_all(right_arr, mesh_name, 0, 0)
+    return jnp.concatenate(z1, axis=0)
+
+
+target_wait = functools.partial(_store_stocks, mesh_name="tp")
 
 
 def from_behind(value, axis, by):
@@ -31,7 +41,7 @@
 def body(tokens, w_query, w_key, w_value, norm_gain):
     local_width = w_query.shape[1]
     head_count = local_width // HEAD_DIM
-    piece_rows = lax.all_gather(tokens, "tp", axis=0, tiled=True)
+    piece_rows = target_wait(tokens)
     query_part = jnp.dot(piece_rows, w_query, preferred_element_type=jnp.float32).astype(
         jnp.bfloat16
     )

time: 132 us -> 123 us (0.932)
  blocking collectives: 0 us -> 42.7 us
  waiting for transfers between devices: 87.1 us -> 48.9 us
  between operations: 13.5 us -> 0.14 us
  matrix products: 14 us -> 12 us
  local copies, waits for them, and re-layouts: 3.27 us -> 4.8 us
    all_to_all x0 -> x1, blocking collectives: none -> 42.7 us  [_store_stocks(): z1 = lax.all_to_all(right_arr, mesh_name, 0, 0)]
    all_gather x1 -> x0, waiting for transfers between devices: 33 us -> none  [body(): piece_rows = lax.all_gather(tokens, 'tp', axis=0, tiled=True)]
    ppermute x5, waiting for transfers between devices: 53.4 us -> 48.9 us  [from_behind(): return lax.ppermute(value, axis, pairs)]
    dot_general x1, matrix products: 3.87 us -> 1.86 us  [body(): jnp.dot(piece_rows, w_value, preferred_element_type=jnp.float32)]
    another operation x0 -> x1, local copies, waits for them, and re-layouts: none -> 1.51 us  [_store_stocks(): right_arr = jnp.stack([z for _ in range(lax.axis_size(mesh_name))], axis=0)]
  transfers between devices with their start and end apart: 6 -> 5, of which waited for: 6 -> 5; matrix products, arithmetic and copies ran while one was open for 3% -> 4% of each run, Pallas kernels for 0% -> 0%
where the time goes in v1:
time: 123 us
  waiting for transfers between devices  48.9 us (40%)
  blocking collectives  42.7 us (35%)
  matrix products  12 us (10%)
  starting transfers between devices  11.7 us (10%)
  local copies, waits for them, and re-layouts  4.8 us (4%)
  other arithmetic  2.71 us (2%)
    ppermute x5, waiting for transfers between devices, from_behind(): return lax.ppermute(value, axis, pairs)  48.9 us
    all_to_all x1, blocking collectives, _store_stocks(): z1 = lax.all_to_all(right_arr, mesh_name, 0, 0)  42.7 us
    ppermute x5, starting transfers between devices, from_behind(): return lax.ppermute(value, axis, pairs)  11.7 us
    dot_general x1, matrix products, body(): jnp.einsum('bhqk,bkhe->bqhe', scores, value_rows, preferred_element_type=...  3.79 us
  transfers between devices with their start and end apart: 5, of which 5 were waited for; matrix products, arithmetic and copies ran while one was open for 4% of the time, Pallas kernels for 0%

profile of v1, /device:TPU:192, one launch (start us, length us, event | category | flops | bytes accessed | tf_op | source)
XLA Modules:
  0.0 123.0 jit_solution(2548392086073541811)
XLA Ops:
  0.0 0.0 copy-start
  0.0 1.5 %stack.2 = bf16[8,64,3072]{2,1,0:T(8,128)(2,1)S(1)} broadcast(bf16[64,3072]{1,0:T(8,128)(2,1)} %param.5), dimensions={1,2} | broadcast | bytes 3538944 | tf_op jit(solution)/shard_map/stack | solution.py:13
  1.5 42.7 %all_to_all.5 = bf16[8,64,3072]{2,1,0:T(8,128)(2,1)S(1)} all-to-all(bf16[8,64,3072]{2,1,0:T(8,128)(2,1)S(1)} %stack.2), channel_id=1, replica_groups=mesh['ctx'=32,'tp'=8] {'tp'}, dimensions={0} | all-to-all | bytes 6291456 | tf_op jit(solution)/shard_map/all_to_all | solution.py:14
  44.2 0.0 copy-done
  44.2 0.0 copy-start.6
  44.2 1.9 %convolution_convert_fusion = bf16[512,512]{0,1:T(8,128)(2,1)S(1)} fusion(bf16[512,3072]{1,0:T(8,128)(2,1)S(1)} %bitcast.30, bf16[3072,512]{1,0:T(8,128)(2,1)S(1)} %copy-done), kind=kOutput, calls=%fused_computation.5 | convolution fusion | flops 1610874880 | bytes 6815744 | tf_op jit(solution)/shard_map/dot_general | solution.py:49
  46.1 0.0 copy-done.6
  46.1 0.0 copy-start.7
  46.1 1.8 %convolution_convert_fusion.1 = bf16[512,512]{0,1:T(8,128)(2,1)S(1)} fusion(bf16[512,3072]{1,0:T(8,128)(2,1)S(1)} %bitcast.31, bf16[3072,512]{1,0:T(8,128)(2,1)S(1)} %copy-done.6), kind=kOutput, calls=%fused_computation.6 | convolution fusion | flops 1610874880 | bytes 6815744 | tf_op jit(solution)/shard_map/dot_general | solution.py:48
  48.0 0.1 copy-done.7
  48.0 1.8 %convolution_convert_fusion.2 = bf16[512,512]{0,1:T(8,128)(2,1)S(1)} fusion(bf16[512,3072]{1,0:T(8,128)(2,1)S(1)} %bitcast.32, bf16[3072,512]{1,0:T(8,128)(2,1)S(1)} %copy-done.7), kind=kOutput, calls=%fused_computation.7 | convolution fusion | flops 1610874880 | bytes 6815744 | tf_op jit(solution)/shard_map/dot_general | solution.py:45
  49.9 0.1 pad_maximum_fusion
  50.0 0.0 copy-start.1
  50.0 1.1 copy-done.1
  51.1 0.3 fusion.2
  51.4 3.4 %collective-permute-start = (f32[4,128,128]{2,1,0:T(8,128)S(1)}, f32[4,128,128]{2,1,0:T(8,128)S(1)}, u32[]{:S(2)}, u32[]{:S(2)}) collective-permute-start(f32[4,128,128]{2,1,0:T(8,128)S(1)} %fusion.2), channel_id=1, source_target_pairs={{0,8},{8,16},{16,24},{24,32},{32,40},{40,48},{48,56},{56,64},{64,7... | collective-permute-start | bytes 786440 | tf_op jit(solution)/shard_map/ppermute | solution.py:24
  54.8 8.3 %collective-permute-done = f32[4,128,128]{2,1,0:T(8,128)S(1)} collective-permute-done((f32[4,128,128]{2,1,0:T(8,128)S(1)}, f32[4,128,128]{2,1,0:T(8,128)S(1)}, u32[]{:S(2)}, u32[]{:S(2)}) %collective-permute-start) | collective-permute-done | bytes 262176 | tf_op jit(solution)/shard_map/ppermute | solution.py:24
  63.1 2.8 %collective-permute-start.1 = (f32[4,128,128]{2,1,0:T(8,128)S(1)}, f32[4,128,128]{2,1,0:T(8,128)S(1)}, u32[]{:S(2)}, u32[]{:S(2)}) collective-permute-start(f32[4,128,128]{2,1,0:T(8,128)S(1)} %add.44), channel_id=1, source_target_pairs={{0,16},{8,24},{16,32},{24,40},{32,48},{40,56},{48,64},{56,72},{64,... | collective-permute-start | bytes 786440 | tf_op jit(solution)/shard_map/ppermute | solution.py:24
  66.0 8.3 %collective-permute-done.1 = f32[4,128,128]{2,1,0:T(8,128)S(1)} collective-permute-done((f32[4,128,128]{2,1,0:T(8,128)S(1)}, f32[4,128,128]{2,1,0:T(8,128)S(1)}, u32[]{:S(2)}, u32[]{:S(2)}) %collective-permute-start.1) | collective-permute-done | bytes 262176 | tf_op jit(solution)/shard_map/ppermute | solution.py:24
  74.3 0.0 copy-start.2
  74.3 2.9 %collective-permute-start.2 = (f32[4,128,128]{2,1,0:T(8,128)S(1)}, f32[4,128,128]{2,1,0:T(8,128)S(1)}, u32[]{:S(2)}, u32[]{:S(2)}) collective-permute-start(f32[4,128,128]{2,1,0:T(8,128)S(1)} %add.46), channel_id=1, source_target_pairs={{0,32},{8,40},{16,48},{24,56},{32,64},{40,72},{48,80},{56,88},{64,... | collective-permute-start | bytes 786440 | tf_op jit(solution)/shard_map/ppermute | solution.py:24
  77.2 5.3 %collective-permute-done.2 = f32[4,128,128]{2,1,0:T(8,128)S(1)} collective-permute-done((f32[4,128,128]{2,1,0:T(8,128)S(1)}, f32[4,128,128]{2,1,0:T(8,128)S(1)}, u32[]{:S(2)}, u32[]{:S(2)}) %collective-permute-start.2) | collective-permute-done | bytes 262176 | tf_op jit(solution)/shard_map/ppermute | solution.py:24
  82.6 0.0 copy-start.3
  82.6 1.3 %collective-permute-start.3 = (f32[4,128,128]{2,1,0:T(8,128)S(1)}, f32[4,128,128]{2,1,0:T(8,128)S(1)}, u32[]{:S(2)}, u32[]{:S(2)}) collective-permute-start(f32[4,128,128]{2,1,0:T(8,128)S(1)} %add.48), channel_id=1, source_target_pairs={{0,64},{8,72},{16,80},{24,88},{32,96},{40,104},{48,112},{56,120},{... | collective-permute-start | bytes 786440 | tf_op jit(solution)/shard_map/ppermute | solution.py:24
  83.9 0.8 iota_compare_fusion
  84.7 13.7 %collective-permute-done.3 = f32[4,128,128]{2,1,0:T(8,128)S(1)} collective-permute-done((f32[4,128,128]{2,1,0:T(8,128)S(1)}, f32[4,128,128]{2,1,0:T(8,128)S(1)}, u32[]{:S(2)}, u32[]{:S(2)}) %collective-permute-start.3) | collective-permute-done | bytes 262176 | tf_op jit(solution)/shard_map/ppermute | solution.py:24
  98.3 0.0 copy-start.4
  98.3 0.8 add.50
  99.1 0.0 copy-done.2
  99.1 0.0 copy-done.3
  99.1 0.0 copy-done.4
  99.1 1.3 %collective-permute-start.4 = (f32[4,128,128]{2,1,0:T(8,128)}, f32[4,128,128]{2,1,0:T(8,128)}, u32[]{:S(2)}, u32[]{:S(2)}) collective-permute-start(f32[4,128,128]{2,1,0:T(8,128)} %add.50), channel_id=1, source_target_pairs={{0,128},{8,136},{16,144},{24,152},{32,160},{40,168},{48,176},{56,1... | collective-permute-start | bytes 786440 | tf_op jit(solution)/shard_map/ppermute | solution.py:24
  100.4 3.8 %fusion = f32[4,128,512]{2,1,0:T(8,128)} fusion(pred[512,512]{1,0:T(8,128)(4,1)} %iota_compare_fusion, bf16[1,512,3,4,128]{1,4,3,2,0:T(8,128)(2,1)} %bitcast.34), kind=kOutput, calls=%fused_computation.1 | convolution fusion | flops 538968064 | bytes 2883584 | tf_op jit(solution)/shard_map/bhqk,bkhe->bqhe/dot_general | solution.py:70
  104.2 0.0 copy-start.5
  104.2 13.3 %collective-permute-done.4 = f32[4,128,128]{2,1,0:T(8,128)} collective-permute-done((f32[4,128,128]{2,1,0:T(8,128)}, f32[4,128,128]{2,1,0:T(8,128)}, u32[]{:S(2)}, u32[]{:S(2)}) %collective-permute-start.4) | collective-permute-done | bytes 262176 | tf_op jit(solution)/shard_map/ppermute | solution.py:24
  117.5 2.4 %multiply_reduce_fusion = (f32[512,4]{0,1:T(4,128)S(1)}, f32[1,512,4,128]{1,3,2,0:T(8,128)S(1)}) fusion(f32[4,128,512]{2,1,0:T(8,128)} %fusion, bf16[1,512,3,4,128]{1,4,3,2,0:T(8,128)(2,1)} %bitcast.35, f32[4,128,128]{2,1,0:T(8,128)} %collective-permute-done.4, f32[4,128,128]{2,1,0:T(8,128)} %copy-done.4, f32[4,128,128]{2,1,0:T(8,128)} %copy-done.3, ...), kind=kOutput, calls=%fused_computation.9 | convolution fusion | flops 403699712 | bytes 3940352 | tf_op jit(solution)/shard_map/bqhd,bhde->bqhe/dot_general | solution.py:71
  120.0 0.0 copy-done.5
  120.0 0.9 multiply_convert_fusion
  120.9 2.0 %copy.9 = bf16[512,512]{1,0:T(8,128)(2,1)} copy(bf16[512,512]{0,1:T(8,128)(2,1)} %bitcast.36) | data formatting | bytes 1048576 | tf_op jit(solution)/shard_map/convert_element_type | solution.py:80
  (4 shorter events, 0.1 us)
Async XLA Ops:
  0.0 44.2 %copy-start = (bf16[3072,512]{1,0:T(8,128)(2,1)S(1)}, bf16[3072,512]{1,0:T(8,128)(2,1)}, u32[]{:S(2)}) copy-start(bf16[3072,512]{1,0:T(8,128)(2,1)} %param.8) | copy-start | bytes 9437188
  44.2 1.9 %copy-start.6 = (bf16[3072,512]{1,0:T(8,128)(2,1)S(1)}, bf16[3072,512]{1,0:T(8,128)(2,1)}, u32[]{:S(2)}) copy-start(bf16[3072,512]{1,0:T(8,128)(2,1)} %param.7) | copy-start | bytes 9437188
  46.1 1.9 %copy-start.7 = (bf16[3072,512]{1,0:T(8,128)(2,1)S(1)}, bf16[3072,512]{1,0:T(8,128)(2,1)}, u32[]{:S(2)}) copy-start(bf16[3072,512]{1,0:T(8,128)(2,1)} %param.6) | copy-start | bytes 9437188
  50.0 1.2 copy-start.1
  51.4 11.7 %collective-permute-start = (f32[4,128,128]{2,1,0:T(8,128)S(1)}, f32[4,128,128]{2,1,0:T(8,128)S(1)}, u32[]{:S(2)}, u32[]{:S(2)}) collective-permute-start(f32[4,128,128]{2,1,0:T(8,128)S(1)} %fusion.2), channel_id=1, source_target_pairs={{0,8},{8,16},{16,24},{24,32},{32,40},{40,48},{48,56},{56,64},{64,7... | collective-permute-start | bytes 786440 | tf_op jit(solution)/shard_map/ppermute | solution.py:24
  63.1 11.1 %collective-permute-start.1 = (f32[4,128,128]{2,1,0:T(8,128)S(1)}, f32[4,128,128]{2,1,0:T(8,128)S(1)}, u32[]{:S(2)}, u32[]{:S(2)}) collective-permute-start(f32[4,128,128]{2,1,0:T(8,128)S(1)} %add.44), channel_id=1, source_target_pairs={{0,16},{8,24},{16,32},{24,40},{32,48},{40,56},{48,64},{56,72},{64,... | collective-permute-start | bytes 786440 | tf_op jit(solution)/shard_map/ppermute | solution.py:24
  74.3 24.9 %copy-start.2 = (f32[4,128,128]{2,1,0:T(8,128)}, f32[4,128,128]{2,1,0:T(8,128)S(1)}, u32[]{:S(2)}) copy-start(f32[4,128,128]{2,1,0:T(8,128)S(1)} %collective-permute-done.1) | copy-start | bytes 786436
  74.3 8.3 %collective-permute-start.2 = (f32[4,128,128]{2,1,0:T(8,128)S(1)}, f32[4,128,128]{2,1,0:T(8,128)S(1)}, u32[]{:S(2)}, u32[]{:S(2)}) collective-permute-start(f32[4,128,128]{2,1,0:T(8,128)S(1)} %add.46), channel_id=1, source_target_pairs={{0,32},{8,40},{16,48},{24,56},{32,64},{40,72},{48,80},{56,88},{64,... | collective-permute-start | bytes 786440 | tf_op jit(solution)/shard_map/ppermute | solution.py:24
  82.6 16.6 %copy-start.3 = (f32[4,128,128]{2,1,0:T(8,128)}, f32[4,128,128]{2,1,0:T(8,128)S(1)}, u32[]{:S(2)}) copy-start(f32[4,128,128]{2,1,0:T(8,128)S(1)} %collective-permute-done.2) | copy-start | bytes 786436
  82.6 15.7 %collective-permute-start.3 = (f32[4,128,128]{2,1,0:T(8,128)S(1)}, f32[4,128,128]{2,1,0:T(8,128)S(1)}, u32[]{:S(2)}, u32[]{:S(2)}) collective-permute-start(f32[4,128,128]{2,1,0:T(8,128)S(1)} %add.48), channel_id=1, source_target_pairs={{0,64},{8,72},{16,80},{24,88},{32,96},{40,104},{48,112},{56,120},{... | collective-permute-start | bytes 786440 | tf_op jit(solution)/shard_map/ppermute | solution.py:24
  98.3 0.8 copy-start.4
  99.1 18.4 %collective-permute-start.4 = (f32[4,128,128]{2,1,0:T(8,128)}, f32[4,128,128]{2,1,0:T(8,128)}, u32[]{:S(2)}, u32[]{:S(2)}) collective-permute-start(f32[4,128,128]{2,1,0:T(8,128)} %add.50), channel_id=1, source_target_pairs={{0,128},{8,136},{16,144},{24,152},{32,160},{40,168},{48,176},{56,1... | collective-permute-start | bytes 786440 | tf_op jit(solution)/shard_map/ppermute | solution.py:24
  104.2 15.8 %copy-start.5 = (f32[512]{0:T(512)S(1)}, f32[512]{0:T(512)}, u32[]{:S(2)}) copy-start(f32[512]{0:T(512)} %param.9) | copy-start | bytes 6148
